TPU v7x, 256 devices: a whole 4x4x8 slice. The times are simulated.
256 devices in a mesh: group: 8 (over x, y_lo), tp: 32 (over z, y_hi, core).
Axes of the slice: x: 4, y: 4 (y_hi: 2, y_lo: 2; y = y_hi * 2 + y_lo), z: 8, core: 2. Of those that a mesh axis runs over, the one named last changes fastest.
Arguments:
- hidden: bfloat16 [2, 256, 8192], P(None, 'group', 'tp'), may hold values from -6 to 6
- query_weight: bfloat16 [8192, 4096], P(None, 'tp'), may hold values from -0.0625 to 0.0625
- key_value_weight: bfloat16 [8192, 1024], P('tp'), may hold values from -0.0625 to 0.0625
- output_weight: bfloat16 [4096, 8192], P('tp'), may hold values from -0.1875 to 0.1875
- adapter_down_weight: bfloat16 [32, 8192, 128], P('group', 'tp'), may hold values from -0.0625 to 0.0625
- adapter_up_query: bfloat16 [32, 64, 4096], P('group', None, 'tp'), may hold values from -0.75 to 0.75
- adapter_up_value: bfloat16 [32, 64, 512], P('group'), may hold values from -0.75 to 0.75
- key_value_pool: bfloat16 [8192, 16, 1024], P(('group', 'tp')), may hold values from -250 to 250
- lengths: int32 [256], P(('group', 'tp')), may hold values from 257 to 512
- request_page_table: int32 [256, 32], P(('group', 'tp')), may hold values from 0 to 63, as said below
- page_send_list: int32 [8, 32, 8, 4], P('group', 'tp'), may hold values from -1 to 31, as said below
- request_adapter_entry: int32 [256], P('group'), may hold values from 0 to 15, as said below
- read_rows_list: int32 [8, 8, 2], replicated, may hold values from -1 to 3, as said below
Outputs:
- layer_out: bfloat16 [2, 256, 8192], P(None, 'group', 'tp')
Inputs may be any that keep to these rules, and one draw needn't show every extreme that they name: `request_page_table`: the entries of one device's requests are distinct; an entry below 32 names a page of that device's pool, an entry 32 + g * 4 + c names slot c of what device (g, same column) lists for this group in page_send_list, and only listed slots are named. `page_send_list`: for each source device and target group the listed pages are distinct and fill the first slots, -1 marks an empty slot; a group lists nothing for itself; in every draw each device fills all 4 slots for some group. `request_adapter_entry`: entry e of a request of group h names slot e % 2 of read_rows_list[h, e // 2], never an empty one; every listed slot is named by some request of the group. `read_rows_list`: listed rows of one reading group and owner are distinct and fill the first slots, -1 marks an empty slot; every reading group reads 2 adapters from some owner.
All inputs are finite; a program needn't handle non-finite values.
Results may differ from a plain program's by a relative error of at most 0.0158.
The roundings to bfloat16 on the way count: a program that leaves them out, or rounds other values in their place, can miss the bound.
Values may be sent and summed in bfloat16 or wider, within the bound.
No kernel may reach another device: no remote copies, remote signals or barrier semaphores. Data moves between devices by JAX's collectives and lax.ppermute only.
A program may use at most 64 MiB of HBM per device.

v0:
```python
import math
import jax
import jax.numpy as jnp
from jax import lax
from jax.sharding import PartitionSpec as P

HEAD_SIZE = 128
QUERY_HEADS = 32
KEY_VALUE_HEADS = 4
ADAPTER_RANK = 64
ADAPTER_SCALE = 1.5


def attend(query_own, ctx_pages, keyval_new, lengths):
    key_span_width = KEY_VALUE_HEADS * HEAD_SIZE
    group_q = QUERY_HEADS // KEY_VALUE_HEADS
    step_count = query_own.shape[0]
    batch_own = query_own.shape[1]
    ctx_len = ctx_pages.shape[1]
    query_rows = query_own.reshape(step_count, batch_own, KEY_VALUE_HEADS, group_q, HEAD_SIZE)
    ctx_keys = ctx_pages[..., :key_span_width].reshape(
        batch_own, ctx_len, KEY_VALUE_HEADS, HEAD_SIZE
    )
    ctx_values = ctx_pages[..., key_span_width:].reshape(
        batch_own, ctx_len, KEY_VALUE_HEADS, HEAD_SIZE
    )
    new_keys = keyval_new[..., :key_span_width].reshape(
        batch_own, step_count, KEY_VALUE_HEADS, HEAD_SIZE
    )
    new_values = keyval_new[..., key_span_width:].reshape(
        batch_own, step_count, KEY_VALUE_HEADS, HEAD_SIZE
    )
    score_scale = 1.0 / math.sqrt(HEAD_SIZE)
    ctx_scores = (
        jnp.einsum("sbkgd,bckd->bkgsc", query_rows, ctx_keys, preferred_element_type=jnp.float32)
        * score_scale
    )
    new_scores = (
        jnp.einsum("sbkgd,btkd->bkgst", query_rows, new_keys, preferred_element_type=jnp.float32)
        * score_scale
    )
    ctx_mask = (jnp.arange(ctx_len)[None, :] < lengths[:, None])[:, None, None, None, :]
    new_mask = jnp.arange(step_count)[None, :] <= jnp.arange(step_count)[:, None]
    ctx_scores = jnp.where(ctx_mask, ctx_scores, -jnp.inf)
    new_scores = jnp.where(new_mask, new_scores, -jnp.inf)
    row_max = jnp.maximum(
        jnp.max(ctx_scores, -1, keepdims=True), jnp.max(new_scores, -1, keepdims=True)
    )
    ctx_weights = jnp.exp(ctx_scores - row_max)
    new_weights = jnp.exp(new_scores - row_max)
    totals = jnp.sum(ctx_weights, -1, keepdims=True) + jnp.sum(new_weights, -1, keepdims=True)
    context = jnp.einsum(
        "bkgsc,bckd->bkgsd",
        ctx_weights.astype(jnp.bfloat16),
        ctx_values,
        preferred_element_type=jnp.float32,
    )
    context = context + jnp.einsum(
        "bkgst,btkd->bkgsd",
        new_weights.astype(jnp.bfloat16),
        new_values,
        preferred_element_type=jnp.float32,
    )
    context = context / totals
    return (
        jnp.transpose(context, (3, 0, 1, 2, 4))
        .reshape(step_count, batch_own, QUERY_HEADS, HEAD_SIZE)
        .astype(jnp.bfloat16)
    )


def per_device(
    hidden,
    query_weight,
    key_value_weight,
    output_weight,
    adapter_down_weight,
    adapter_up_query,
    adapter_up_value,
    key_value_pool,
    lengths,
    request_page_table,
    page_send_list,
    request_adapter_entry,
    read_rows_list,
):
    group_number = lax.axis_index("group")
    column_id = lax.axis_index("tp")
    step_count, batch_rows, width_local = hidden.shape
    batch_own = lengths.shape[0]
    key_span_width = KEY_VALUE_HEADS * HEAD_SIZE
    cap_slots = read_rows_list.shape[2]
    holder_group = request_adapter_entry // cap_slots
    slot_column = request_adapter_entry % cap_slots
    own_start = column_id * batch_own
    whole_down, whole_upq, whole_upv = (
        lax.all_gather(adapter_down_weight, "group", axis=0, tiled=True),
        lax.all_gather(adapter_up_query, "group", axis=0, tiled=True),
        lax.all_gather(adapter_up_value, "group", axis=0, tiled=True),
    )
    storage_rows = (
        holder_group * adapter_down_weight.shape[0]
        + read_rows_list[group_number, holder_group, slot_column]
    )
    down_rows = jnp.take(whole_down, storage_rows, axis=0)
    upq_rows = jnp.take(whole_upq, storage_rows, axis=0)
    upv_rows = jnp.take(
        whole_upv, lax.dynamic_slice_in_dim(storage_rows, own_start, batch_own), axis=0
    )
    shrink_part = jnp.einsum("srd,rdk->srk", hidden, down_rows, preferred_element_type=jnp.float32)
    down_projected_low = lax.psum(shrink_part, "tp").astype(jnp.bfloat16)
    query_plain = jnp.einsum(
        "srd,dc->src",
        lax.all_gather(hidden, "tp", axis=2, tiled=True),
        query_weight,
        preferred_element_type=jnp.float32,
    )
    query_adapter_term = jnp.einsum(
        "srk,rkc->src",
        down_projected_low[..., :ADAPTER_RANK],
        upq_rows,
        preferred_element_type=jnp.float32,
    )
    query_rows = (query_plain + ADAPTER_SCALE * query_adapter_term).astype(jnp.bfloat16)
    key_value_plain = lax.psum_scatter(
        jnp.einsum("srd,dc->rsc", hidden, key_value_weight, preferred_element_type=jnp.float32),
        "tp",
        scatter_dimension=0,
        tiled=True,
    )
    shrink_own = lax.dynamic_slice_in_dim(down_projected_low, own_start, batch_own, 1)
    value_adapter_term = ADAPTER_SCALE * jnp.einsum(
        "srk,rkc->rsc", shrink_own[..., ADAPTER_RANK:], upv_rows, preferred_element_type=jnp.float32
    )
    keyval_new = jnp.concatenate(
        [
            key_value_plain[..., :key_span_width],
            key_value_plain[..., key_span_width:] + value_adapter_term,
        ],
        -1,
    ).astype(jnp.bfloat16)
    heads_local = query_rows.shape[2] // HEAD_SIZE
    query_own = lax.all_to_all(
        query_rows.reshape(step_count, batch_rows, heads_local, HEAD_SIZE),
        "tp",
        split_axis=1,
        concat_axis=2,
        tiled=True,
    )
    move_row = page_send_list[0, 0]
    present_pages = (move_row >= 0).reshape(-1)
    outgoing = (
        jnp.take(key_value_pool, jnp.maximum(move_row, 0).reshape(-1), axis=0)
        * present_pages.astype(key_value_pool.dtype)[:, None, None]
    )
    arrived_pages = lax.all_to_all(outgoing, "group", split_axis=0, concat_axis=0, tiled=True)
    combined = jnp.concatenate([key_value_pool, arrived_pages], 0)
    ctx_pages = jnp.take(combined, request_page_table.reshape(-1), axis=0).reshape(
        batch_own, -1, 2 * key_span_width
    )
    attended = attend(query_own, ctx_pages, keyval_new, lengths)
    heads_back = lax.all_to_all(attended, "tp", split_axis=2, concat_axis=1, tiled=True)
    projected = jnp.dot(
        heads_back.reshape(step_count * batch_rows, -1),
        output_weight,
        preferred_element_type=jnp.float32,
    )
    summed = lax.psum_scatter(
        projected.reshape(step_count, batch_rows, -1), "tp", scatter_dimension=2, tiled=True
    )
    return summed.astype(jnp.bfloat16)


def solution(mesh):
    placed = (
        P(None, "group", "tp"),
        P(None, "tp"),
        P("tp", None),
        P("tp", None),
        P("group", "tp", None),
        P("group", None, "tp"),
        P("group", None, None),
        P(("group", "tp"), None, None),
        P(("group", "tp")),
        P(("group", "tp"), None),
        P("group", "tp", None, None),
        P("group"),
        P(),
    )
    return jax.shard_map(
        per_device, mesh=mesh, in_specs=placed, out_specs=P(None, "group", "tp"), check_vma=False
    )
```

profile of v0, /device:TPU:6, one launch (start us, length us, event | category | flops | bytes accessed | tf_op | source)
XLA Modules:
  0.0 627.6 jit_solution(2606935624223614851)
XLA Ops:
  6.5 0.7 all-gather.6.cloned.1.call-update
  7.3 0.7 all-gather.4.cloned.1.call-update
  8.1 1.2 convolution_bitcast_fusion
  9.3 0.9 copy.70
  10.3 0.7 compare_convert_fusion
  11.0 0.7 broadcast_maximum_fusion
  12.2 1.8 gather_fusion
  14.1 1.1 select_multiply_fusion
  15.2 6.5 %all-to-all-start = ((bf16[32,16,1024]{2,1,0:T(8,128)(2,1)}), bf16[32,16,1024]{2,1,0:T(8,128)(2,1)}, u32[]{:S(2)}, u32[]{:S(2)}) async-start(bf16[32,16,1024]{2,1,0:T(8,128)(2,1)} %select_multiply_fusion), calls=%async_computation | async-start | bytes 2097152 | tf_op jit(solution)/shard_map/all_to_all | solution.py:156
  22.3 0.8 gather_fusion.2
  24.0 0.6 dynamic_slice.7
  26.6 47.8 %all_gather.13 = bf16[32,64,128]{2,1,0:T(8,128)(2,1)} all-gather(bf16[4,64,128]{2,1,0:T(8,128)(2,1)S(1)} %copy-done.4), channel_id=1, replica_groups=mesh['group'=8,'tp'=32] {'group'}, dimensions={0}, use_global_device_ids=true | all-gather | bytes 589824 | tf_op jit(solution)/shard_map/all_gather | solution.py:98
  74.4 2.5 gather_fusion.3
  77.5 2.7 pad_maximum_fusion
  80.2 2.2 gather_fusion.1
  82.4 1.3 copy.63
  83.8 1.3 broadcast_select_fusion
  85.2 3.7 gather_fusion.4
  88.9 2.0 fusion.10
  91.0 134.4 %psum.7 = bf16[2,32,128]{2,0,1:T(2,128)(2,1)S(1)} all-reduce(f32[2,32,128]{2,0,1:T(2,128)S(1)} %fusion.10), channel_id=1, replica_groups=mesh['group'=8,'tp'=32] {'tp'}, use_global_device_ids=true, to_apply=%region_0.1 | all-reduce | flops 8192 | bytes 49152 | tf_op jit(solution)/shard_map/psum | solution.py:111
  225.4 1.3 fusion.31
  226.7 2.4 fusion.21
  229.2 0.6 copy.66
  229.8 3.8 all-to-all-start.1
  233.7 196.1 %all-reduce.3.cloned.1.call-done = f32[32,2,1024]{2,1,0:T(2,128)} async-done(((f32[32,2,1024]{2,1,0:T(2,128)}), f32[32,2,1024]{2,1,0:T(2,128)}) %all-reduce.3.cloned.1.call-update) | async-done | bytes 262160
  429.8 1.5 convolution_multiply_fusion.1
  432.2 51.4 %all-gather.8.cloned.1.call-done = bf16[32,64,512]{2,1,0:T(8,128)(2,1)} async-done(((bf16[4,64,512]{2,1,0:T(8,128)(2,1)}), bf16[32,64,512]{2,1,0:T(8,128)(2,1)}) %all-gather.8.cloned.1.call-update) | async-done | bytes 2097168 | tf_op jit(solution)/shard_map/all_gather | solution.py:99
  483.6 1.8 fusion.24
  485.4 19.1 %all_to_all.23 = bf16[2,1,32,128]{3,0,1,2:T(2,128)(2,1)S(1)} all-to-all(bf16[2,1,32,128]{3,0,1,2:T(2,128)(2,1)S(1)} %copy.79), channel_id=1, replica_groups=mesh['group'=8,'tp'=32] {'tp'}, dimensions={2} | all-to-all | bytes 32768 | tf_op jit(solution)/shard_map/all_to_all | solution.py:162
  504.5 1.8 fusion
  506.3 113.3 %reduce-scatter.2.cloned.1.call-done = f32[2,32,256]{2,1,0:T(8,128)} async-done(((f32[2,32,8192]{2,1,0:T(8,128)}), f32[2,32,256]{2,1,0:T(8,128)}) %reduce-scatter.2.cloned.1.call-update) | async-done | bytes 65552 | tf_op jit(solution)/shard_map/reduce_scatter | solution.py:168
  619.6 1.5 convert_element_type.64
  (58 shorter events, 3.2 us)
Async XLA Ops:
  6.5 498.0 %copy-start = (bf16[128,8192]{1,0:T(8,128)(2,1)S(1)}, bf16[128,8192]{1,0:T(8,128)(2,1)}, u32[]{:S(2)}) copy-start(bf16[128,8192]{1,0:T(8,128)(2,1)} %param.16) | copy-start | bytes 6291460
  6.5 78.7 %all-gather.6.cloned.1.call-start = ((), (), s32[]{:S(2)}) async-start(), calls=%async_computation.5 | async-start | bytes 2359296 | tf_op jit(solution)/shard_map/all_gather | solution.py:97
  7.3 219.5 %all-gather.4.cloned.1.call-start = ((), (), s32[]{:S(2)}) async-start(), calls=%async_computation.4 | async-start | bytes 1081344 | tf_op jit(solution)/shard_map/all_gather | solution.py:114
  8.0 421.8 %all-reduce.3.cloned.1.call-start = ((), (), s32[]{:S(2)}) async-start(), calls=%async_computation.8 | async-start | bytes 524288
  14.0 8.3 %copy-start.5 = (s32[32]{0:T(128)S(1)}, s32[32]{0:T(128)}, u32[]{:S(2)}) copy-start(s32[32]{0:T(128)} %param.24) | copy-start | bytes 388
  14.0 8.3 %copy-start.1 = (s32[8,8,2]{1,2,0:T(2,128)S(1)}, s32[8,8,2]{1,2,0:T(2,128)}, u32[]{:S(2)}) copy-start(s32[8,8,2]{1,2,0:T(2,128)} %param.25) | copy-start | bytes 1540
  14.1 9.1 %copy-start.6 = (s32[1,32]{1,0:T(1,128)S(1)}, s32[1,32]{1,0:T(1,128)}, u32[]{:S(2)}) copy-start(s32[1,32]{1,0:T(1,128)} %param.22) | copy-start | bytes 388
  14.1 12.5 %copy-start.4 = (bf16[4,64,128]{2,1,0:T(8,128)(2,1)S(1)}, bf16[4,64,128]{2,1,0:T(8,128)(2,1)}, u32[]{:S(2)}) copy-start(bf16[4,64,128]{2,1,0:T(8,128)(2,1)} %param.18) | copy-start | bytes 196612
  15.2 61.6 %copy-start.7 = (u32[256]{0:T(256)S(1)}, u32[256]{0:T(256)}, u32[]{:S(2)}) copy-start(u32[256]{0:T(256)} %constant.176) | copy-start | bytes 3076
  15.2 62.3 %copy-start.2 = (bf16[32,16,1024]{2,1,0:T(8,128)(2,1)S(1)}, bf16[32,16,1024]{2,1,0:T(8,128)(2,1)}, u32[]{:S(2)}) copy-start(bf16[32,16,1024]{2,1,0:T(8,128)(2,1)} %param.20) | copy-start | bytes 3145732
  15.2 62.2 %all-to-all-start = ((bf16[32,16,1024]{2,1,0:T(8,128)(2,1)}), bf16[32,16,1024]{2,1,0:T(8,128)(2,1)}, u32[]{:S(2)}, u32[]{:S(2)}) async-start(bf16[32,16,1024]{2,1,0:T(8,128)(2,1)} %select_multiply_fusion), calls=%async_computation | async-start | bytes 2097152 | tf_op jit(solution)/shard_map/all_to_all | solution.py:156
  21.7 461.9 %all-gather.8.cloned.1.call-start = ((), (), s32[]{:S(2)}) async-start(), calls=%async_computation.6 | async-start | bytes 2359296 | tf_op jit(solution)/shard_map/all_gather | solution.py:99
  85.2 3.8 copy-start.3
  229.8 200.0 %all-to-all-start.1 = ((bf16[2,32,1,128]{3,0,2,1:T(2,128)(2,1)}), bf16[2,32,1,128]{3,0,2,1:T(2,128)(2,1)S(1)}, u32[]{:S(2)}, u32[]{:S(2)}) async-start(bf16[2,32,1,128]{3,0,2,1:T(2,128)(2,1)} %copy.66), calls=%async_computation.1 | async-start | bytes 32768 | tf_op jit(solution)/shard_map/all_to_all | solution.py:143
  233.6 386.0 %reduce-scatter.2.cloned.1.call-start = ((), (), s32[]{:S(2)}) async-start(), calls=%async_computation.7 | async-start | bytes 2162688 | tf_op jit(solution)/shard_map/reduce_scatter | solution.py:168
Sparse Core Ops, SparseCore 0:
  9.1 74.8 all-gather.5
  86.6 76.9 all-gather.3
  166.2 263.5 all-reduce.2
  431.6 52.0 all-gather.7
  506.4 113.1 reduce-scatter.1
where the time goes:
time: 628 us
  waiting for transfers between devices  363 us (58%)
  blocking collectives  201 us (32%)
  local copies, waits for them, and re-layouts  16 us (3%)
  between operations  16 us (3%)
  matrix products  12.6 us (2%)
  starting transfers between devices  10.5 us (2%)
  other arithmetic  8.48 us (1%)
    unnamed x6, waiting for transfers between devices  198 us
    psum x1, blocking collectives, per_device(): down_projected_low = lax.psum(shrink_part, 'tp').astype(jnp.bfloat16)  134 us
    reduce_scatter x1, waiting for transfers between devices, per_device(): lax.psum_scatter(projected.reshape(step_count, batch_rows, -1), 'tp', sca...  113 us
    all_gather x1, waiting for transfers between devices, per_device(): lax.all_gather(adapter_up_value, 'group', axis=0, tiled=True)  51.4 us
    all_gather x1, blocking collectives, per_device(): lax.all_gather(adapter_up_query, 'group', axis=0, tiled=True)  47.8 us
    all_to_all x1, blocking collectives, per_device(): lax.all_to_all(attended, 'tp', split_axis=2, concat_axis=1, tiled=True)  19.1 us
  transfers between devices with their start and end apart: 7, of which 3 were waited for; matrix products, arithmetic and copies ran while one was open for 5% of the time, Pallas kernels for 0%

commit v1 on v0

--- a/solution.py
+++ b/solution.py
@@ -1,3 +1,4 @@
+import functools
 import math
 import jax
 import jax.numpy as jnp
@@ -9,6 +10,13 @@
 KEY_VALUE_HEADS = 4
 ADAPTER_RANK = 64
 ADAPTER_SCALE = 1.5
+
+
+def report_indices(mine_x, ax_name):
+    return jnp.sum(lax.all_gather(mine_x, axis_name=ax_name), axis=0)
+
+
+_step_on_regions = functools.partial(report_indices, ax_name="tp")
 
 
 def attend(query_own, ctx_pages, keyval_new, lengths):
@@ -108,7 +116,7 @@
         whole_upv, lax.dynamic_slice_in_dim(storage_rows, own_start, batch_own), axis=0
     )
     shrink_part = jnp.einsum("srd,rdk->srk", hidden, down_rows, preferred_element_type=jnp.float32)
-    down_projected_low = lax.psum(shrink_part, "tp").astype(jnp.bfloat16)
+    down_projected_low = _step_on_regions(shrink_part).astype(jnp.bfloat16)
     query_plain = jnp.einsum(
         "srd,dc->src",
         lax.all_gather(hidden, "tp", axis=2, tiled=True),

time: 628 us -> 691 us (1.10)
  waiting for transfers between devices: 363 us -> 567 us
  blocking collectives: 201 us -> 56.4 us
    psum x1 -> x0, blocking collectives: 134 us -> none  [per_device(): down_projected_low = lax.psum(shrink_part, 'tp').astype(jnp.bfloat16)]
    all_gather x1, waiting for transfers between devices: 0.02 us -> 68.9 us  [per_device(): lax.all_gather(hidden, 'tp', axis=2, tiled=True)]
    unnamed x6 -> x7, waiting for transfers between devices: 198 us -> 259 us
    all_gather x1, waiting for transfers between devices: 0.02 us -> 55.5 us  [per_device(): lax.all_gather(adapter_down_weight, 'group', axis=0, tiled=True)]
    all_gather x0 -> x1, waiting for transfers between devices: none -> 19.6 us  [report_indices(): return jnp.sum(lax.all_gather(mine_x, axis_name=ax_name), axis=0)]
    all_gather x1, blocking collectives: 47.8 us -> 37.3 us  [per_device(): lax.all_gather(adapter_up_query, 'group', axis=0, tiled=True)]
  transfers between devices with their start and end apart: 7 -> 8, of which waited for: 3 -> 6; matrix products, arithmetic and copies ran while one was open for 5% -> 4% of each run, Pallas kernels for 0% -> 0%
where the time goes in v1:
time: 691 us; the launch traced here: 690 us
  waiting for transfers between devices  567 us (82%)
  blocking collectives  56.4 us (8%)
  local copies, waits for them, and re-layouts  17.3 us (3%)
  between operations  16 us (2%)
  starting transfers between devices  12.4 us (2%)
  matrix products  11.5 us (2%)
  other arithmetic  9.08 us (1%)
    unnamed x7, waiting for transfers between devices  259 us
    reduce_scatter x1, waiting for transfers between devices, per_device(): lax.psum_scatter(projected.reshape(step_count, batch_rows, -1), 'tp', sca...  113 us
    all_gather x1, waiting for transfers between devices, per_device(): lax.all_gather(hidden, 'tp', axis=2, tiled=True)  68.9 us
    all_gather x1, waiting for transfers between devices, per_device(): lax.all_gather(adapter_down_weight, 'group', axis=0, tiled=True)  55.5 us
    all_gather x1, waiting for transfers between devices, per_device(): lax.all_gather(adapter_up_value, 'group', axis=0, tiled=True)  51.5 us
    all_gather x1, blocking collectives, per_device(): lax.all_gather(adapter_up_query, 'group', axis=0, tiled=True)  37.3 us
    all_gather x1, waiting for transfers between devices, report_indices(): return jnp.sum(lax.all_gather(mine_x, axis_name=ax_name), axis=0)  19.6 us
    all_to_all x1, blocking collectives, per_device(): lax.all_to_all(attended, 'tp', split_axis=2, concat_axis=1, tiled=True)  19.1 us
  transfers between devices with their start and end apart: 8, of which 6 were waited for; matrix products, arithmetic and copies ran while one was open for 4% of the time, Pallas kernels for 0%

profile of v1, /device:TPU:6, one launch (start us, length us, event | category | flops | bytes accessed | tf_op | source)
XLA Modules:
  0.0 690.0 jit_solution(8702371679187426277)
XLA Ops:
  6.5 0.7 all-gather.8.cloned.1.call-update
  7.3 0.7 fusion.65
  8.0 1.5 gather_fusion.2
  9.5 55.5 %all-gather.8.cloned.1.call-done = bf16[32,256,128]{2,1,0:T(8,128)(2,1)} async-done(((bf16[4,256,128]{2,1,0:T(8,128)(2,1)}), bf16[32,256,128]{2,1,0:T(8,128)(2,1)}) %all-gather.8.cloned.1.call-update) | async-done | bytes 2097168 | tf_op jit(solution)/shard_map/all_gather | solution.py:105
  65.0 3.7 gather_fusion.4
  68.8 2.1 fusion.10
  70.9 0.6 copy.88
  71.6 0.7 all-gather.6.cloned.1.call-update
  72.6 0.9 copy.95
  74.7 1.8 gather_fusion
  76.6 1.1 select_multiply_fusion
  77.7 5.8 all-to-all-start
  83.5 37.3 %all_gather.19 = bf16[32,64,128]{2,1,0:T(8,128)(2,1)} all-gather(bf16[4,64,128]{2,1,0:T(8,128)(2,1)S(1)} %copy-done.5), channel_id=1, replica_groups=mesh['group'=8,'tp'=32] {'group'}, dimensions={0}, use_global_device_ids=true | all-gather | bytes 589824 | tf_op jit(solution)/shard_map/all_gather | solution.py:106
  120.8 2.5 gather_fusion.3
  126.9 2.7 pad_maximum_fusion
  129.7 2.2 gather_fusion.1
  131.9 1.3 copy.86
  133.2 1.3 broadcast_select_fusion
  134.6 19.6 %all-gather.12.cloned.1.call-done = f32[64,32,128]{2,1,0:T(8,128)} async-done(((f32[2,32,128]{2,1,0:T(8,128)}), f32[64,32,128]{2,1,0:T(8,128)}) %all-gather.12.cloned.1.call-update) | async-done | bytes 1048592 | tf_op jit(solution)/shard_map/all_gather | solution.py:16
  154.3 1.3 reduce_sum.27
  155.6 1.3 fusion.31
  156.9 68.9 %all-gather.6.cloned.1.call-done = bf16[2,32,8192]{2,1,0:T(8,128)(2,1)} async-done(((bf16[2,32,256]{2,1,0:T(8,128)(2,1)}), bf16[2,32,8192]{2,1,0:T(8,128)(2,1)}) %all-gather.6.cloned.1.call-update) | async-done | bytes 1048592 | tf_op jit(solution)/shard_map/all_gather | solution.py:122
  225.8 2.4 fusion.21
  228.8 6.4 all-to-all-start.1
  235.3 256.7 %all-reduce.3.cloned.1.call-done = f32[32,2,1024]{2,1,0:T(2,128)} async-done(((f32[32,2,1024]{2,1,0:T(2,128)}), f32[32,2,1024]{2,1,0:T(2,128)}) %all-reduce.3.cloned.1.call-update) | async-done | bytes 262160
  492.0 1.4 convolution_multiply_fusion.1
  494.4 51.5 %all-gather.10.cloned.1.call-done = bf16[32,64,512]{2,1,0:T(8,128)(2,1)} async-done(((bf16[4,64,512]{2,1,0:T(8,128)(2,1)}), bf16[32,64,512]{2,1,0:T(8,128)(2,1)}) %all-gather.10.cloned.1.call-update) | async-done | bytes 2097168 | tf_op jit(solution)/shard_map/all_gather | solution.py:107
  545.8 1.7 fusion.24
  547.6 19.1 %all_to_all.23 = bf16[2,1,32,128]{3,0,1,2:T(2,128)(2,1)S(1)} all-to-all(bf16[2,1,32,128]{3,0,1,2:T(2,128)(2,1)S(1)} %copy.104), channel_id=1, replica_groups=mesh['group'=8,'tp'=32] {'tp'}, dimensions={2} | all-to-all | bytes 32768 | tf_op jit(solution)/shard_map/all_to_all | solution.py:170
  566.7 1.8 fusion
  568.5 113.3 %reduce-scatter.2.cloned.1.call-done = f32[2,32,256]{2,1,0:T(8,128)} async-done(((f32[2,32,8192]{2,1,0:T(8,128)}), f32[2,32,256]{2,1,0:T(8,128)}) %reduce-scatter.2.cloned.1.call-update) | async-done | bytes 65552 | tf_op jit(solution)/shard_map/reduce_scatter | solution.py:176
  681.7 1.5 convert_element_type.64
  (65 shorter events, 4.6 us)
Async XLA Ops:
  6.5 560.2 %copy-start = (bf16[128,8192]{1,0:T(8,128)(2,1)S(1)}, bf16[128,8192]{1,0:T(8,128)(2,1)}, u32[]{:S(2)}) copy-start(bf16[128,8192]{1,0:T(8,128)(2,1)} %param.16) | copy-start | bytes 6291460
  6.5 58.5 %all-gather.8.cloned.1.call-start = ((), (), s32[]{:S(2)}) async-start(), calls=%async_computation.5 | async-start | bytes 2359296 | tf_op jit(solution)/shard_map/all_gather | solution.py:105
  7.3 147.0 %all-gather.12.cloned.1.call-start = ((), (), s32[]{:S(2)}) async-start(), calls=%async_computation.8 | async-start | bytes 1081344 | tf_op jit(solution)/shard_map/all_gather | solution.py:16
  9.5 59.3 %copy-start.3 = (bf16[2,32,256]{2,1,0:T(8,128)(2,1)S(1)}, bf16[2,32,256]{2,1,0:T(8,128)(2,1)}, u32[]{:S(2)}) copy-start(bf16[2,32,256]{2,1,0:T(8,128)(2,1)} %param.13) | copy-start | bytes 98308
  68.8 3.6 copy-start.2
  68.8 3.6 copy-start.4
  68.8 5.3 copy-start.6
  71.5 154.2 %all-gather.6.cloned.1.call-start = ((), (), s32[]{:S(2)}) async-start(), calls=%async_computation.4 | async-start | bytes 1081344 | tf_op jit(solution)/shard_map/all_gather | solution.py:122
  72.3 419.7 %all-reduce.3.cloned.1.call-start = ((), (), s32[]{:S(2)}) async-start(), calls=%async_computation.9 | async-start | bytes 524288
  73.5 472.3 %all-gather.10.cloned.1.call-start = ((), (), s32[]{:S(2)}) async-start(), calls=%async_computation.6 | async-start | bytes 2359296 | tf_op jit(solution)/shard_map/all_gather | solution.py:107
  76.6 6.9 %copy-start.5 = (bf16[4,64,128]{2,1,0:T(8,128)(2,1)S(1)}, bf16[4,64,128]{2,1,0:T(8,128)(2,1)}, u32[]{:S(2)}) copy-start(bf16[4,64,128]{2,1,0:T(8,128)(2,1)} %param.18) | copy-start | bytes 196612
  77.7 45.5 %copy-start.7 = (s32[1,32]{1,0:T(1,128)S(1)}, s32[1,32]{1,0:T(1,128)}, u32[]{:S(2)}) copy-start(s32[1,32]{1,0:T(1,128)} %param.22) | copy-start | bytes 388
  77.7 48.6 %copy-start.8 = (u32[256]{0:T(256)S(1)}, u32[256]{0:T(256)}, u32[]{:S(2)}) copy-start(u32[256]{0:T(256)} %constant.176) | copy-start | bytes 3076
  77.7 49.2 %copy-start.1 = (bf16[32,16,1024]{2,1,0:T(8,128)(2,1)S(1)}, bf16[32,16,1024]{2,1,0:T(8,128)(2,1)}, u32[]{:S(2)}) copy-start(bf16[32,16,1024]{2,1,0:T(8,128)(2,1)} %param.20) | copy-start | bytes 3145732
  77.7 49.2 %all-to-all-start = ((bf16[32,16,1024]{2,1,0:T(8,128)(2,1)}), bf16[32,16,1024]{2,1,0:T(8,128)(2,1)}, u32[]{:S(2)}, u32[]{:S(2)}) async-start(bf16[32,16,1024]{2,1,0:T(8,128)(2,1)} %select_multiply_fusion), calls=%async_computation | async-start | bytes 2097152 | tf_op jit(solution)/shard_map/all_to_all | solution.py:164
  228.8 263.2 %all-to-all-start.1 = ((bf16[2,32,1,128]{3,0,2,1:T(2,128)(2,1)}), bf16[2,32,1,128]{3,0,2,1:T(2,128)(2,1)S(1)}, u32[]{:S(2)}, u32[]{:S(2)}) async-start(bf16[2,32,1,128]{3,0,2,1:T(2,128)(2,1)} %copy.91), calls=%async_computation.1 | async-start | bytes 32768 | tf_op jit(solution)/shard_map/all_to_all | solution.py:151
  235.2 446.5 %reduce-scatter.2.cloned.1.call-start = ((), (), s32[]{:S(2)}) async-start(), calls=%async_computation.7 | async-start | bytes 2162688 | tf_op jit(solution)/shard_map/reduce_scatter | solution.py:176
Sparse Core Ops, SparseCore 0:
  9.1 55.8 all-gather.7
  71.7 82.5 all-gather.11
  156.8 68.9 all-gather.5
  228.2 263.7 all-reduce.2
  493.8 52.0 all-gather.9
  568.6 113.0 reduce-scatter.1
